TPU v7x, 128 devices: a whole 4x4x4 slice. The times are simulated.
128 devices in a mesh: req: 8 (over x, core), seq: 16 (over z, y).
Axes of the slice: x: 4, y: 4, z: 4, core: 2. Of those that a mesh axis runs over, the one named last changes fastest.
Arguments:
- hidden: bfloat16 [8, 2048, 2048], P('req', 'seq'), may hold values from -6 to 6
- lengths: int32 [8], replicated, may hold values from 1 to 2048, 10240 in all
- slot_request: int32 [8], replicated, may hold values from 0 to 7, each once
- norm_gain: bfloat16 [2048], replicated, may hold values from 0.099609375 to 1.8984375
- in_weight: bfloat16 [2, 2048, 4096], P(None, 'req', 'seq'), may hold values from -0.125 to 0.125
- conv_weight: bfloat16 [4, 4096], P(None, 'seq'), may hold values from -3 to 3
- conv_bias: bfloat16 [4096], P('seq'), may hold values from -0.5 to 0.5
- xproj_weight: bfloat16 [4096, 160], P('seq'), may hold values from -0.09375 to 0.09375
- dt_weight: bfloat16 [128, 4096], P(None, 'seq'), may hold values from -0.5 to 0.5
- dt_bias: bfloat16 [4096], P('seq'), may hold values from -6.91 to -2.25
- a_log: float32 [16, 4096], replicated, may hold values from -2.3 to 1.39
- skip_gain: float32 [4096], replicated, may hold values from 0.5 to 1.5
- out_weight: bfloat16 [4096, 2048], P('seq', 'req'), may hold values from -0.09375 to 0.09375
Outputs:
- mixed: bfloat16 [8, 2048, 2048], P('req', 'seq')
- final_state: float32 [8, 16, 4096], P('req', None, 'seq')
Inputs may be any that keep to these rules, and one draw needn't show every extreme that they name: `lengths`: each slot's length is at least 1, the longest is exactly 2048, and they sum to 10240. `slot_request`: A permutation of the requests.
All inputs are finite; a program needn't handle non-finite values.
Results may differ from a plain program's by a relative error of at most 0.015.
Values may be sent and summed in bfloat16 or wider, within the bound.
No kernel may reach another device: no remote copies, remote signals or barrier semaphores. Data moves between devices by JAX's collectives and lax.ppermute only.
A program may use at most 128 MiB of HBM per device.

v0:
```python
import jax
import jax.numpy as jnp
from jax import lax
from jax.sharding import PartitionSpec as P

STATE = 16
RANK = 128


def shifted(block, axis, distance):
    devices = range(lax.axis_size(axis))
    route = [(i - distance, i) for i in devices if i - distance in devices]
    return lax.ppermute(block, axis, route)


def spread(array, axis, root):
    mine = lax.axis_index(axis) == root
    return lax.psum(jnp.where(mine, array, jnp.zeros_like(array)), axis)


def to_blocks(array):
    pieces, length, columns = array.shape
    return jnp.moveaxis(array.reshape(pieces, 16, length // 16, columns), 1, 0)


def from_blocks(array):
    count, pieces, group, columns = array.shape
    return jnp.moveaxis(array, 0, 1).reshape(pieces, count * group, columns)


def piece_scan(rates, values, entry, readout, decay):
    pieces, length, columns = rates.shape
    group = length // 16
    positions = jnp.arange(length, dtype=jnp.int32)
    lower = (positions[None, :] <= positions[:, None]).astype(jnp.float32)
    running = jnp.einsum("rs,psw->prw", lower, rates, precision=lax.Precision.HIGHEST)

    def advance(state, items):
        rate, value, into, outof = items
        outputs = []
        for place in range(group):
            factor = jnp.exp(rate[:, place][:, None, :] * decay[None])
            state = (
                factor * state
                + (rate[:, place] * value[:, place])[:, None, :] * into[:, place][:, :, None]
            )
            outputs.append(jnp.sum(outof[:, place][:, :, None] * state, axis=1))
        return (state, jnp.stack(outputs, axis=1))

    start = jnp.zeros((pieces, decay.shape[0], columns), jnp.float32)
    end_local, local_out = lax.scan(
        advance, start, (to_blocks(rates), to_blocks(values), to_blocks(entry), to_blocks(readout))
    )
    total_decay = jnp.exp(running[:, length - 1][:, None, :] * decay[None])
    return (end_local, from_blocks(local_out), total_decay, running)


def carried_part(running, readout, decay, carry_in):

    def correct(items):
        total, outof = items
        kept = jnp.exp(total[:, :, None, :] * decay[None, None]) * carry_in[:, None]
        return jnp.sum(outof[:, :, :, None] * kept, axis=2)

    return from_blocks(lax.map(correct, (to_blocks(running), to_blocks(readout))))


def per_device(
    hidden,
    lengths,
    slot_request,
    norm_gain,
    in_weight,
    conv_weight,
    conv_bias,
    xproj_weight,
    dt_weight,
    dt_bias,
    a_log,
    skip_gain,
    out_weight,
):
    seq_count = lax.axis_size("seq")
    seq_index = lax.axis_index("seq")
    req_index = lax.axis_index("req")
    rows = hidden.shape[1]
    span = rows * seq_count
    width = in_weight.shape[2]
    taps_count = conv_weight.shape[0]
    state_count = a_log.shape[0]
    total_inner = a_log.shape[1]
    tokens = hidden[0].astype(jnp.float32)
    scale = lax.rsqrt(jnp.mean(tokens * tokens, axis=-1, keepdims=True) + 1e-05)
    normed = (tokens * scale * norm_gain.astype(jnp.float32)).astype(jnp.bfloat16)
    w_in = lax.all_gather(in_weight, "req", axis=1, tiled=True)
    w_flat = jnp.concatenate((w_in[0], w_in[1]), axis=1)
    both = jnp.dot(
        lax.all_gather(normed, "seq", axis=0, tiled=True),
        w_flat,
        preferred_element_type=jnp.float32,
    )
    xin = both[:, :width]
    zgate = both[:, width:].astype(jnp.bfloat16)
    padded = jnp.pad(xin, ((taps_count - 1, 0), (0, 0)))
    taps = conv_weight.astype(jnp.float32)
    convolved = conv_bias.astype(jnp.float32) + jnp.zeros_like(xin)
    for tap in range(taps_count):
        convolved = convolved + taps[tap] * padded[tap : tap + span, :]
    inner = jax.nn.silu(convolved).astype(jnp.bfloat16)
    partial_proj = jnp.dot(inner, xproj_weight, preferred_element_type=jnp.float32)
    length_here = lax.dynamic_index_in_dim(lengths, req_index, 0, keepdims=False)
    summed = lax.psum(partial_proj, "seq")
    live_all = (jnp.arange(span, dtype=jnp.int32) < length_here).astype(jnp.float32)
    rate_low = summed[:, :RANK].astype(jnp.bfloat16)
    delta_ch = (
        jax.nn.softplus(
            jnp.dot(rate_low, dt_weight, preferred_element_type=jnp.float32)
            + dt_bias.astype(jnp.float32)
        )
        * live_all[:, None]
    )
    w_out = lax.all_gather(out_weight, "req", axis=1, tiled=True)
    inner_tok = lax.all_to_all(inner, "seq", split_axis=0, concat_axis=1, tiled=True)
    delta_tok = lax.all_to_all(
        delta_ch.astype(jnp.bfloat16), "seq", split_axis=0, concat_axis=1, tiled=True
    ).astype(delta_ch.dtype)
    own_proj = lax.dynamic_slice_in_dim(summed, seq_index * rows, rows, 0)
    decay = -jnp.exp(a_log)
    inner_f = inner_tok.astype(jnp.float32)
    entry = own_proj[None, :, RANK : RANK + STATE]
    readout = own_proj[None, :, RANK + STATE :]
    end_local, local_out, total_decay, running = piece_scan(
        delta_tok[None], inner_f[None], entry, readout, decay
    )
    zeros_state = jnp.zeros((state_count, total_inner), jnp.float32)

    def relay(turn, incoming):
        return shifted(total_decay[0] * incoming + end_local[0], "seq", 1)

    carry_in = lax.fori_loop(0, seq_count - 1, relay, zeros_state)
    carried = carried_part(running, readout, decay, carry_in[None])
    scanned = ((local_out + carried)[0] + skip_gain * inner_f).astype(jnp.bfloat16)
    last = spread(
        (total_decay[0] * carry_in + end_local[0]).astype(jnp.bfloat16), "seq", seq_count - 1
    ).astype(jnp.float32)
    mine = lax.dynamic_slice_in_dim(last, seq_index * width, width, 1)
    scanned_ch = lax.all_to_all(scanned, "seq", split_axis=1, concat_axis=0, tiled=True)
    gated_ch = (scanned_ch.astype(jnp.float32) * jax.nn.silu(zgate.astype(jnp.float32))).astype(
        jnp.bfloat16
    )
    branch = lax.psum_scatter(
        jnp.dot(gated_ch, w_out, preferred_element_type=jnp.float32).astype(jnp.bfloat16),
        "seq",
        scatter_dimension=0,
        tiled=True,
    ).astype(jnp.float32)
    slot_all = lax.all_gather(mine[None], "req", axis=0, tiled=True)
    picked = (slot_request == req_index).astype(jnp.float32)
    final_state = jnp.sum(picked[:, None, None] * slot_all, axis=0, keepdims=True)
    mixed = (tokens + branch).astype(jnp.bfloat16)[None]
    return (mixed, final_state)


def solution(mesh):
    in_specs = (
        P("req", "seq", None),
        P(),
        P(),
        P(),
        P(None, "req", "seq"),
        P(None, "seq"),
        P("seq"),
        P("seq", None),
        P(None, "seq"),
        P("seq"),
        P(),
        P(),
        P("seq", "req"),
    )
    out_specs = (P("req", "seq", None), P("req", None, "seq"))
    return jax.shard_map(
        per_device, mesh=mesh, in_specs=in_specs, out_specs=out_specs, check_vma=False
    )
```

profile of v0, /device:TPU:0, one launch (start us, length us, event | category | flops | bytes accessed | tf_op | source)
XLA Modules:
  0.0 717.7 jit_solution(14593859675135900258)
XLA Ops:
  12.1 25.4 %all-gather.7.cloned.1.call-done = bf16[2,2048,256]{2,1,0:T(8,128)(2,1)} async-done(((bf16[2,256,256]{2,1,0:T(8,128)(2,1)}), bf16[2,2048,256]{2,1,0:T(8,128)(2,1)}) %all-gather.7.cloned.1.call-update) | async-done | bytes 2097168 | tf_op jit(solution)/shard_map/all_gather | solution.py:95
  39.2 72.3 %all-gather.5.cloned.1.call-done = bf16[2048,2048]{1,0:T(8,128)(2,1)} async-done(((bf16[128,2048]{1,0:T(8,128)(2,1)}), bf16[2048,2048]{1,0:T(8,128)(2,1)}) %all-gather.5.cloned.1.call-update) | async-done | bytes 8388624 | tf_op jit(solution)/shard_map/all_gather | solution.py:98
  111.5 6.9 fusion.33
  122.7 2.8 fusion.56
  125.5 5.4 all-to-all-start.1
  132.2 88.7 %all-reduce.4.cloned.1.call-done = f32[2048,160]{0,1:T(8,128)} async-done(((f32[2048,160]{0,1:T(8,128)}), f32[2048,160]{0,1:T(8,128)}) %all-reduce.4.cloned.1.call-update) | async-done | bytes 1310736 | tf_op jit(solution)/shard_map/psum | solution.py:112
  220.9 2.7 fusion.32
  225.0 5.1 all-to-all-start
  234.1 2.8 reshape.994
  238.4 7.5 %all-to-all-done = bf16[16,128,256]{1,2,0:T(8,128)(2,1)S(1)} async-done(((bf16[16,128,256]{1,2,0:T(8,128)(2,1)}), bf16[16,128,256]{1,2,0:T(8,128)(2,1)S(1)}, u32[]{:S(2)}, u32[]{:S(2)}) %all-to-all-start) | async-done | bytes 1048608 | tf_op jit(solution)/shard_map/all_to_all | solution.py:124
  255.7 65.7 %while.35 = (s32[]{:T(128)}, f32[1,16,4096]{2,1,0:T(8,128)S(1)}, f32[16,1,8,4096]{3,2,1,0:T(8,128)}, f32[16,1,8,4096]{3,2,1,0:T(8,128)}, f32[16,4096]{1,0:T(8,12...) while((s32[]{:T(128)}, f32[1,16,4096]{2,1,0:T(8,128)S(1)}, ...), condition=%wide.region_11.12_spmd.clone, body=%wide.region_2.11_spmd.clone.sunk | while | flops 4849667 | bytes 4347896 | solution.py:51
  321.5 148.6 %while.33 = (s32[]{:T(128)}, f32[16,4096]{1,0:T(8,128)S(1)}, f32[1,16,4096]{2,1,0:T(8,128)S(1)}, f32[1,16,4096]{2,1,0:T(8,128)S(1)}, s32[]{:T(128)}) while((s32[]{:T(128)}, f32[16,4096]{1,0:T(8,128)S(1)}, f32[1,16,4096]{2,1,0:T(8,128)S(1)}, f32[1,16,4096]{2,1,0:T(8,128)S(1)}, s32[]{:T(128)}) %tuple.124), condition=%wide.region_13.14_spmd, body=%wide.region_12.13_spmd.sunk | while | flops 131074 | bytes 2097253 | solution.py:140
  324.1 3.9 collective-permute-done
  328.0 4.4 collective-permute-start
  332.4 5.0 collective-permute-done
  337.4 4.4 collective-permute-start
  341.8 6.1 collective-permute-done
  347.9 4.4 collective-permute-start
  352.4 6.1 collective-permute-done
  358.5 4.4 collective-permute-start
  362.9 5.2 collective-permute-done
  368.1 4.4 collective-permute-start
  372.5 4.3 collective-permute-done
  376.9 4.4 collective-permute-start
  381.3 3.9 collective-permute-done
  385.2 6.8 collective-permute-start
  392.1 5.6 collective-permute-done
  397.7 6.2 collective-permute-start
  404.0 4.5 collective-permute-done
  408.5 5.6 collective-permute-start
  414.1 3.9 collective-permute-done
  418.0 6.5 collective-permute-start
  424.5 3.9 collective-permute-done
  428.4 6.5 collective-permute-start
  435.0 3.9 collective-permute-done
  438.9 6.5 collective-permute-start
  445.4 3.9 collective-permute-done
  449.3 6.5 collective-permute-start
  455.8 3.9 collective-permute-done
  459.7 6.5 collective-permute-start
  466.2 3.9 collective-permute-done
  471.6 35.8 %while.34 = (s32[]{:T(128)}, f32[16,1,8,4096]{3,2,1,0:T(8,128)}, f32[16,1,8,16]{3,2,1,0:T(8,128)S(1)}, f32[16,1,8,4096]{3,2,1,0:T(8,128)}, f32[16,4096]{1,0:T(8,128)S(1)}, /*index=5*/f32[16,4096]{1,0:T(8,128)S(1)}, s32[]{:T(128)}) while((s32[]{:T(128)}, f32[16,1,8,4096]{3,2,1,0:T(8,128)}, f32[16,1,8,16]{3,2,1,0:T(8,128)S(1)}, ...), condition=%wide.region_16.17_spmd, body=%wide.region_14.16_spmd.sunk | while | flops 2064386 | bytes 1312853 | solution.py:65
  512.9 18.0 %all-to-all-start.2 = ((bf16[128,16,256]{2,0,1:T(8,128)(2,1)}), bf16[128,16,256]{2,0,1:T(8,128)(2,1)S(1)}, u32[]{:S(2)}, u32[]{:S(2)}) async-start(bf16[128,16,256]{2,0,1:T(8,128)(2,1)} %fusion.30), calls=%async_computation.2 | async-start | bytes 2097152 | tf_op jit(solution)/shard_map/all_to_all | solution.py:147
  532.1 12.2 %all-to-all-done.2 = bf16[128,16,256]{2,0,1:T(8,128)(2,1)S(1)} async-done(((bf16[128,16,256]{2,0,1:T(8,128)(2,1)}), bf16[128,16,256]{2,0,1:T(8,128)(2,1)S(1)}, u32[]{:S(2)}, u32[]{:S(2)}) %all-to-all-start.2) | async-done | bytes 1048608 | tf_op jit(solution)/shard_map/all_to_all | solution.py:147
  546.7 6.8 convolution_convert_fusion
  554.1 66.1 %all-reduce.6.cloned.1.call-done = bf16[16,4096]{1,0:T(8,128)(2,1)} async-done(((bf16[16,4096]{1,0:T(8,128)(2,1)}), bf16[16,4096]{1,0:T(8,128)(2,1)}) %all-reduce.6.cloned.1.call-update) | async-done | bytes 131088 | tf_op jit(solution)/shard_map/psum | solution.py:18
  620.9 13.0 %all-gather = f32[128,256]{1,0:T(8,128)S(1)} all-gather(f32[16,256]{1,0:T(8,128)S(1)} %dynamic-slice_convert_fusion), channel_id=2, replica_groups=mesh['req'=8,'seq'=16] {'req'}, dimensions={0}, use_global_device_ids=true | all-gather | bytes 147456 | tf_op jit(solution)/shard_map/all_gather | solution.py:157
  634.6 74.3 %reduce-scatter.2.cloned.1.call-done = bf16[128,2048]{1,0:T(8,128)(2,1)} async-done(((bf16[2048,2048]{1,0:T(8,128)(2,1)}), bf16[128,2048]{1,0:T(8,128)(2,1)}) %reduce-scatter.2.cloned.1.call-update) | async-done | bytes 524304 | tf_op jit(solution)/shard_map/reduce_scatter | solution.py:151
  (340 shorter events, 146.6 us)
Async XLA Ops:
  7.2 115.5 %copy-start = (bf16[256,160]{0,1:T(8,128)(2,1)S(1)}, bf16[256,160]{0,1:T(8,128)(2,1)}, u32[]{:S(2)}) copy-start(bf16[256,160]{0,1:T(8,128)(2,1)} %param.26) | copy-start | bytes 245764
  7.2 4.8 copy-start.12
  7.2 4.8 copy-start.10
  7.2 30.3 %all-gather.7.cloned.1.call-start = ((), (), s32[]{:S(2)}) async-start(), calls=%async_computation.5 | async-start | bytes 2359296 | tf_op jit(solution)/shard_map/all_gather | solution.py:95
  7.9 103.6 %all-gather.5.cloned.1.call-start = ((), (), s32[]{:S(2)}) async-start(), calls=%async_computation.4 | async-start | bytes 8912896 | tf_op jit(solution)/shard_map/all_gather | solution.py:98
  12.0 209.0 %all-reduce.4.cloned.1.call-start = ((), (), s32[]{:S(2)}) async-start(), calls=%async_computation.6 | async-start | bytes 2621440 | tf_op jit(solution)/shard_map/psum | solution.py:112
  118.4 2.0 copy-start.4
  125.5 5.5 copy-start.13
  125.5 5.5 copy-start.14
  125.5 95.4 %copy-start.11 = (bf16[128,256]{1,0:T(8,128)(2,1)S(1)}, bf16[128,256]{1,0:T(8,128)(2,1)}, u32[]{:S(2)}) copy-start(bf16[128,256]{1,0:T(8,128)(2,1)} %param.27) | copy-start | bytes 196612
  125.5 99.5 %all-to-all-start.1 = ((bf16[16,128,256]{2,1,0:T(8,128)(2,1)}), bf16[16,128,256]{2,1,0:T(8,128)(2,1)S(1)}, u32[]{:S(2)}, u32[]{:S(2)}) async-start(bf16[16,128,256]{2,1,0:T(8,128)(2,1)} %bitcast.17), calls=%async_computation.1 | async-start | bytes 2097152 | tf_op jit(solution)/shard_map/all_to_all | solution.py:123
  223.6 7.1 copy-start.9
  225.0 20.9 %all-to-all-start = ((bf16[16,128,256]{1,2,0:T(8,128)(2,1)}), bf16[16,128,256]{1,2,0:T(8,128)(2,1)S(1)}, u32[]{:S(2)}, u32[]{:S(2)}) async-start(bf16[16,128,256]{1,2,0:T(8,128)(2,1)} %copy.43), calls=%async_computation | async-start | bytes 2097152 | tf_op jit(solution)/shard_map/all_to_all | solution.py:124
  230.1 316.6 %all-gather.9.cloned.1.call-start = ((), (), s32[]{:S(2)}) async-start(), calls=%async_computation.7 | async-start | bytes 1179648 | tf_op jit(solution)/shard_map/all_gather | solution.py:122
  246.3 1.3 copy-start.3
  247.7 5.4 copy-start.6
  321.5 6.4 collective-permute-start
  328.0 9.4 %collective-permute-start = (f32[16,4096]{1,0:T(8,128)S(1)}, f32[16,4096]{1,0:T(8,128)S(1)}, u32[]{:S(2)}, u32[]{:S(2)}) collective-permute-start(f32[16,4096]{1,0:T(8,128)S(1)} %bitcast_add_fusion.3), channel_id=1, source_target_pairs={{0,1},{1,2},{2,3},{3,4},{4,5},{5,6},{6,7},{7,8},{8,9},{9,10},{10,1... | collective-permute-start | bytes 786440 | tf_op jit(solution)/shard_map/while/body/eval_jaxpr/ppermute | solution.py:13
  337.4 10.5 %collective-permute-start = (f32[16,4096]{1,0:T(8,128)S(1)}, f32[16,4096]{1,0:T(8,128)S(1)}, u32[]{:S(2)}, u32[]{:S(2)}) collective-permute-start(f32[16,4096]{1,0:T(8,128)S(1)} %bitcast_add_fusion.3), channel_id=1, source_target_pairs={{0,1},{1,2},{2,3},{3,4},{4,5},{5,6},{6,7},{7,8},{8,9},{9,10},{10,1... | collective-permute-start | bytes 786440 | tf_op jit(solution)/shard_map/while/body/eval_jaxpr/ppermute | solution.py:13
  347.9 10.5 %collective-permute-start = (f32[16,4096]{1,0:T(8,128)S(1)}, f32[16,4096]{1,0:T(8,128)S(1)}, u32[]{:S(2)}, u32[]{:S(2)}) collective-permute-start(f32[16,4096]{1,0:T(8,128)S(1)} %bitcast_add_fusion.3), channel_id=1, source_target_pairs={{0,1},{1,2},{2,3},{3,4},{4,5},{5,6},{6,7},{7,8},{8,9},{9,10},{10,1... | collective-permute-start | bytes 786440 | tf_op jit(solution)/shard_map/while/body/eval_jaxpr/ppermute | solution.py:13
  358.5 9.6 %collective-permute-start = (f32[16,4096]{1,0:T(8,128)S(1)}, f32[16,4096]{1,0:T(8,128)S(1)}, u32[]{:S(2)}, u32[]{:S(2)}) collective-permute-start(f32[16,4096]{1,0:T(8,128)S(1)} %bitcast_add_fusion.3), channel_id=1, source_target_pairs={{0,1},{1,2},{2,3},{3,4},{4,5},{5,6},{6,7},{7,8},{8,9},{9,10},{10,1... | collective-permute-start | bytes 786440 | tf_op jit(solution)/shard_map/while/body/eval_jaxpr/ppermute | solution.py:13
  368.1 8.8 %collective-permute-start = (f32[16,4096]{1,0:T(8,128)S(1)}, f32[16,4096]{1,0:T(8,128)S(1)}, u32[]{:S(2)}, u32[]{:S(2)}) collective-permute-start(f32[16,4096]{1,0:T(8,128)S(1)} %bitcast_add_fusion.3), channel_id=1, source_target_pairs={{0,1},{1,2},{2,3},{3,4},{4,5},{5,6},{6,7},{7,8},{8,9},{9,10},{10,1... | collective-permute-start | bytes 786440 | tf_op jit(solution)/shard_map/while/body/eval_jaxpr/ppermute | solution.py:13
  376.9 8.3 %collective-permute-start = (f32[16,4096]{1,0:T(8,128)S(1)}, f32[16,4096]{1,0:T(8,128)S(1)}, u32[]{:S(2)}, u32[]{:S(2)}) collective-permute-start(f32[16,4096]{1,0:T(8,128)S(1)} %bitcast_add_fusion.3), channel_id=1, source_target_pairs={{0,1},{1,2},{2,3},{3,4},{4,5},{5,6},{6,7},{7,8},{8,9},{9,10},{10,1... | collective-permute-start | bytes 786440 | tf_op jit(solution)/shard_map/while/body/eval_jaxpr/ppermute | solution.py:13
  385.2 12.5 %collective-permute-start = (f32[16,4096]{1,0:T(8,128)S(1)}, f32[16,4096]{1,0:T(8,128)S(1)}, u32[]{:S(2)}, u32[]{:S(2)}) collective-permute-start(f32[16,4096]{1,0:T(8,128)S(1)} %bitcast_add_fusion.3), channel_id=1, source_target_pairs={{0,1},{1,2},{2,3},{3,4},{4,5},{5,6},{6,7},{7,8},{8,9},{9,10},{10,1... | collective-permute-start | bytes 786440 | tf_op jit(solution)/shard_map/while/body/eval_jaxpr/ppermute | solution.py:13
  397.7 10.7 %collective-permute-start = (f32[16,4096]{1,0:T(8,128)S(1)}, f32[16,4096]{1,0:T(8,128)S(1)}, u32[]{:S(2)}, u32[]{:S(2)}) collective-permute-start(f32[16,4096]{1,0:T(8,128)S(1)} %bitcast_add_fusion.3), channel_id=1, source_target_pairs={{0,1},{1,2},{2,3},{3,4},{4,5},{5,6},{6,7},{7,8},{8,9},{9,10},{10,1... | collective-permute-start | bytes 786440 | tf_op jit(solution)/shard_map/while/body/eval_jaxpr/ppermute | solution.py:13
  408.5 9.5 %collective-permute-start = (f32[16,4096]{1,0:T(8,128)S(1)}, f32[16,4096]{1,0:T(8,128)S(1)}, u32[]{:S(2)}, u32[]{:S(2)}) collective-permute-start(f32[16,4096]{1,0:T(8,128)S(1)} %bitcast_add_fusion.3), channel_id=1, source_target_pairs={{0,1},{1,2},{2,3},{3,4},{4,5},{5,6},{6,7},{7,8},{8,9},{9,10},{10,1... | collective-permute-start | bytes 786440 | tf_op jit(solution)/shard_map/while/body/eval_jaxpr/ppermute | solution.py:13
  418.0 10.4 %collective-permute-start = (f32[16,4096]{1,0:T(8,128)S(1)}, f32[16,4096]{1,0:T(8,128)S(1)}, u32[]{:S(2)}, u32[]{:S(2)}) collective-permute-start(f32[16,4096]{1,0:T(8,128)S(1)} %bitcast_add_fusion.3), channel_id=1, source_target_pairs={{0,1},{1,2},{2,3},{3,4},{4,5},{5,6},{6,7},{7,8},{8,9},{9,10},{10,1... | collective-permute-start | bytes 786440 | tf_op jit(solution)/shard_map/while/body/eval_jaxpr/ppermute | solution.py:13
  428.4 10.4 %collective-permute-start = (f32[16,4096]{1,0:T(8,128)S(1)}, f32[16,4096]{1,0:T(8,128)S(1)}, u32[]{:S(2)}, u32[]{:S(2)}) collective-permute-start(f32[16,4096]{1,0:T(8,128)S(1)} %bitcast_add_fusion.3), channel_id=1, source_target_pairs={{0,1},{1,2},{2,3},{3,4},{4,5},{5,6},{6,7},{7,8},{8,9},{9,10},{10,1... | collective-permute-start | bytes 786440 | tf_op jit(solution)/shard_map/while/body/eval_jaxpr/ppermute | solution.py:13
  438.9 10.4 %collective-permute-start = (f32[16,4096]{1,0:T(8,128)S(1)}, f32[16,4096]{1,0:T(8,128)S(1)}, u32[]{:S(2)}, u32[]{:S(2)}) collective-permute-start(f32[16,4096]{1,0:T(8,128)S(1)} %bitcast_add_fusion.3), channel_id=1, source_target_pairs={{0,1},{1,2},{2,3},{3,4},{4,5},{5,6},{6,7},{7,8},{8,9},{9,10},{10,1... | collective-permute-start | bytes 786440 | tf_op jit(solution)/shard_map/while/body/eval_jaxpr/ppermute | solution.py:13
  449.3 10.4 %collective-permute-start = (f32[16,4096]{1,0:T(8,128)S(1)}, f32[16,4096]{1,0:T(8,128)S(1)}, u32[]{:S(2)}, u32[]{:S(2)}) collective-permute-start(f32[16,4096]{1,0:T(8,128)S(1)} %bitcast_add_fusion.3), channel_id=1, source_target_pairs={{0,1},{1,2},{2,3},{3,4},{4,5},{5,6},{6,7},{7,8},{8,9},{9,10},{10,1... | collective-permute-start | bytes 786440 | tf_op jit(solution)/shard_map/while/body/eval_jaxpr/ppermute | solution.py:13
  459.7 10.4 %collective-permute-start = (f32[16,4096]{1,0:T(8,128)S(1)}, f32[16,4096]{1,0:T(8,128)S(1)}, u32[]{:S(2)}, u32[]{:S(2)}) collective-permute-start(f32[16,4096]{1,0:T(8,128)S(1)} %bitcast_add_fusion.3), channel_id=1, source_target_pairs={{0,1},{1,2},{2,3},{3,4},{4,5},{5,6},{6,7},{7,8},{8,9},{9,10},{10,1... | collective-permute-start | bytes 786440 | tf_op jit(solution)/shard_map/while/body/eval_jaxpr/ppermute | solution.py:13
  509.9 0.7 copy-start.8
  512.9 18.1 %copy-start.5 = (f32[16,4096]{1,0:T(8,128)S(1)}, f32[16,4096]{1,0:T(8,128)}, u32[]{:S(2)}) copy-start(f32[16,4096]{1,0:T(8,128)} %param.29) | copy-start | bytes 786436
  512.9 18.1 %copy-start.7 = (f32[1,1,4096]{2,1,0:T(1,128)S(1)}, f32[1,1,4096]{2,1,0:T(1,128)}, u32[]{:S(2)}) copy-start(f32[1,1,4096]{2,1,0:T(1,128)} %copy-done.6) | copy-start | bytes 49156
  512.9 31.4 %all-to-all-start.2 = ((bf16[128,16,256]{2,0,1:T(8,128)(2,1)}), bf16[128,16,256]{2,0,1:T(8,128)(2,1)S(1)}, u32[]{:S(2)}, u32[]{:S(2)}) async-start(bf16[128,16,256]{2,0,1:T(8,128)(2,1)} %fusion.30), calls=%async_computation.2 | async-start | bytes 2097152 | tf_op jit(solution)/shard_map/all_to_all | solution.py:147
  531.0 89.2 %all-reduce.6.cloned.1.call-start = ((), (), s32[]{:S(2)}) async-start(), calls=%async_computation.9 | async-start | bytes 262144 | tf_op jit(solution)/shard_map/psum | solution.py:18
  531.8 177.1 %reduce-scatter.2.cloned.1.call-start = ((), (), s32[]{:S(2)}) async-start(), calls=%async_computation.8 | async-start | bytes 8912896 | tf_op jit(solution)/shard_map/reduce_scatter | solution.py:151
  553.5 0.7 copy-start.15
  553.5 155.5 %copy-start.2 = (bf16[1,128,2048]{2,1,0:T(8,128)(2,1)S(1)}, bf16[1,128,2048]{2,1,0:T(8,128)(2,1)}, u32[]{:S(2)}) copy-start(bf16[1,128,2048]{2,1,0:T(8,128)(2,1)} %param.19) | copy-start | bytes 1572868
  553.5 157.4 %copy-start.1 = (bf16[256,160]{0,1:T(8,128)(2,1)S(1)}, bf16[256,160]{0,1:T(8,128)(2,1)}, u32[]{:S(2)}) copy-start(bf16[256,160]{0,1:T(8,128)(2,1)} %param.26) | copy-start | bytes 245764
Sparse Core Ops, SparseCore 0:
  9.7 27.7 all-gather.6
  40.2 71.2 all-gather.4
  125.6 95.2 all-reduce.3
  232.3 24.7 all-gather.8
  535.2 84.9 all-reduce.5
  623.5 85.3 reduce-scatter.1
where the time goes:
time: 720 us; the launch traced here: 718 us
  waiting for transfers between devices  415 us (58%)
  starting transfers between devices  109 us (15%)
  local copies, waits for them, and re-layouts  89.9 us (12%)
  other arithmetic  54.7 us (8%)
  matrix products  19.6 us (3%)
  between operations  14.4 us (2%)
  blocking collectives  13 us (2%)
    psum x1, waiting for transfers between devices, per_device(): summed = lax.psum(partial_proj, 'seq')  88.7 us
    ppermute x15, starting transfers between devices, shifted(): return lax.ppermute(block, axis, route)  80.1 us
    reduce_scatter x1, waiting for transfers between devices, per_device(): lax.psum_scatter(jnp.dot(gated_ch, w_out, preferred_element_type=jnp.floa...  74.3 us
    all_gather x1, waiting for transfers between devices, per_device(): lax.all_gather(normed, 'seq', axis=0, tiled=True)  72.3 us
    ppermute x15, waiting for transfers between devices, shifted(): return lax.ppermute(block, axis, route)  67.6 us
    psum x1, waiting for transfers between devices, spread(): return lax.psum(jnp.where(mine, array, jnp.zeros_like(array)), axis)  66.1 us
    squeeze x32, local copies, waits for them, and re-layouts, piece_scan(): lax.scan(advance, start, (to_blocks(rates), to_blocks(values), to_blocks(...  26.9 us
    all_gather x1, waiting for transfers between devices, per_device(): w_in = lax.all_gather(in_weight, 'req', axis=1, tiled=True)  25.4 us
  transfers between devices with their start and end apart: 24, of which 22 were waited for; matrix products, arithmetic and copies ran while one was open for 20% of the time, Pallas kernels for 0%

commit v1 on v0

--- a/solution.py
+++ b/solution.py
@@ -109,7 +109,19 @@
     inner = jax.nn.silu(convolved).astype(jnp.bfloat16)
     partial_proj = jnp.dot(inner, xproj_weight, preferred_element_type=jnp.float32)
     length_here = lax.dynamic_index_in_dim(lengths, req_index, 0, keepdims=False)
-    summed = lax.psum(partial_proj, "seq")
+
+    def wrap_yards(array_in):
+        world_n = lax.axis_size("seq")
+        local_part = array_in
+        for c in [at for at in (1, 2, 4, 8, 16) if at < world_n]:
+            v1 = range(world_n)
+            local_now = map(lambda b: (b, b ^ c), v1)
+            z_new = list(local_now)
+            carry_out = lax.ppermute(local_part, "seq", z_new)
+            local_part = local_part + carry_out
+        return local_part
+
+    summed = wrap_yards(partial_proj)
     live_all = (jnp.arange(span, dtype=jnp.int32) < length_here).astype(jnp.float32)
     rate_low = summed[:, :RANK].astype(jnp.bfloat16)
     delta_ch = (

time: 720 us -> 748 us (1.039)
  waiting for transfers between devices: 415 us -> 443 us
  starting transfers between devices: 109 us -> 121 us
  local copies, waits for them, and re-layouts: 89.9 us -> 80 us
    ppermute x0 -> x4, waiting for transfers between devices: none -> 115 us  [wrap_yards(): carry_out = lax.ppermute(local_part, 'seq', z_new)]
    psum x1 -> x0, waiting for transfers between devices: 88.7 us -> none  [per_device(): summed = lax.psum(partial_proj, 'seq')]
    squeeze x32, local copies, waits for them, and re-layouts: 26.9 us -> 15.9 us  [piece_scan(): lax.scan(advance, start, (to_blocks(rates), to_blocks(values), to_blocks(...]
    ppermute x0 -> x4, starting transfers between devices: none -> 9.09 us  [wrap_yards(): carry_out = lax.ppermute(local_part, 'seq', z_new)]
  transfers between devices with their start and end apart: 24 -> 27, of which waited for: 22 -> 25; matrix products, arithmetic and copies ran while one was open for 20% -> 18% of each run, Pallas kernels for 0% -> 0%
where the time goes in v1:
time: 748 us; the launch traced here: 746 us
  waiting for transfers between devices  443 us (59%)
  starting transfers between devices  121 us (16%)
  local copies, waits for them, and re-layouts  80 us (11%)
  other arithmetic  55.7 us (7%)
  matrix products  17.3 us (2%)
  between operations  14.1 us (2%)
  blocking collectives  13 us (2%)
    ppermute x4, waiting for transfers between devices, wrap_yards(): carry_out = lax.ppermute(local_part, 'seq', z_new)  115 us
    ppermute x15, starting transfers between devices, shifted(): return lax.ppermute(block, axis, route)  84.6 us
    reduce_scatter x1, waiting for transfers between devices, per_device(): lax.psum_scatter(jnp.dot(gated_ch, w_out, preferred_element_type=jnp.floa...  74.4 us
    all_gather x1, waiting for transfers between devices, per_device(): lax.all_gather(normed, 'seq', axis=0, tiled=True)  72.3 us
    ppermute x15, waiting for transfers between devices, shifted(): return lax.ppermute(block, axis, route)  69.6 us
    psum x1, waiting for transfers between devices, spread(): return lax.psum(jnp.where(mine, array, jnp.zeros_like(array)), axis)  65.8 us
    all_gather x1, waiting for transfers between devices, per_device(): w_in = lax.all_gather(in_weight, 'req', axis=1, tiled=True)  25.5 us
    dynamic_update_slice x32, local copies, waits for them, and re-layouts, piece_scan(): lax.scan(advance, start, (to_blocks(rates), to_blocks(values), to_blocks(...  21.3 us
  transfers between devices with their start and end apart: 27, of which 25 were waited for; matrix products, arithmetic and copies ran while one was open for 18% of the time, Pallas kernels for 0%

profile of v1, /device:TPU:0, one launch (start us, length us, event | category | flops | bytes accessed | tf_op | source)
XLA Modules:
  0.0 746.0 jit_solution(4297703062251797324)
XLA Ops:
  12.0 25.5 %all-gather.7.cloned.1.call-done = bf16[2,2048,256]{2,1,0:T(8,128)(2,1)} async-done(((bf16[2,256,256]{2,1,0:T(8,128)(2,1)}), bf16[2,2048,256]{2,1,0:T(8,128)(2,1)}) %all-gather.7.cloned.1.call-update) | async-done | bytes 2097168 | tf_op jit(solution)/shard_map/all_gather | solution.py:95
  39.2 72.3 %all-gather.5.cloned.1.call-done = bf16[2048,2048]{1,0:T(8,128)(2,1)} async-done(((bf16[128,2048]{1,0:T(8,128)(2,1)}), bf16[2048,2048]{1,0:T(8,128)(2,1)}) %all-gather.5.cloned.1.call-update) | async-done | bytes 8388624 | tf_op jit(solution)/shard_map/all_gather | solution.py:98
  111.5 6.9 fusion.33
  126.0 28.9 %collective-permute-done.1 = f32[2048,160]{0,1:T(8,128)S(1)} collective-permute-done((f32[2048,160]{0,1:T(8,128)S(1)}, f32[2048,160]{0,1:T(8,128)S(1)}, u32[]{:S(2)}, u32[]{:S(2)}) %collective-permute-start.1) | collective-permute-done | bytes 1310752 | tf_op jit(solution)/shard_map/ppermute | solution.py:120
  158.1 28.0 %collective-permute-done.2 = f32[2048,160]{0,1:T(8,128)S(1)} collective-permute-done((f32[2048,160]{0,1:T(8,128)S(1)}, f32[2048,160]{0,1:T(8,128)S(1)}, u32[]{:S(2)}, u32[]{:S(2)}) %collective-permute-start.2) | collective-permute-done | bytes 1310752 | tf_op jit(solution)/shard_map/ppermute | solution.py:120
  187.7 27.3 %collective-permute-done.3 = f32[2048,160]{0,1:T(8,128)S(1)} collective-permute-done((f32[2048,160]{0,1:T(8,128)S(1)}, f32[2048,160]{0,1:T(8,128)S(1)}, u32[]{:S(2)}, u32[]{:S(2)}) %collective-permute-start.3) | collective-permute-done | bytes 1310752 | tf_op jit(solution)/shard_map/ppermute | solution.py:120
  218.2 4.6 all-to-all-start.1
  224.1 31.2 %collective-permute-done.4 = f32[2048,160]{0,1:T(8,128)} collective-permute-done((f32[2048,160]{0,1:T(8,128)S(1)}, f32[2048,160]{0,1:T(8,128)}, u32[]{:S(2)}, u32[]{:S(2)}) %collective-permute-start.4) | collective-permute-done | bytes 1310752 | tf_op jit(solution)/shard_map/ppermute | solution.py:120
  259.6 5.4 all-to-all-start
  272.2 6.5 all-to-all-done
  289.7 55.2 %while.35 = (s32[]{:T(128)}, f32[1,16,4096]{2,1,0:T(8,128)S(1)}, f32[16,1,8,4096]{3,2,1,0:T(8,128)}, f32[16,1,8,4096]{3,2,1,0:T(8,128)}, f32[16,4096]{1,0:T(8,12...) while((s32[]{:T(128)}, f32[1,16,4096]{2,1,0:T(8,128)S(1)}, ...), condition=%wide.region_10.11_spmd.clone, body=%wide.region_1.10_spmd.clone.sunk | while | flops 4849667 | bytes 4347896 | solution.py:51
  344.9 155.0 %while.33 = (s32[]{:T(128)}, f32[16,4096]{1,0:T(8,128)S(1)}, f32[1,16,4096]{2,1,0:T(8,128)S(1)}, f32[1,16,4096]{2,1,0:T(8,128)S(1)}, s32[]{:T(128)}) while((s32[]{:T(128)}, f32[16,4096]{1,0:T(8,128)S(1)}, f32[1,16,4096]{2,1,0:T(8,128)S(1)}, f32[1,16,4096]{2,1,0:T(8,128)S(1)}, s32[]{:T(128)}) %tuple.124), condition=%wide.region_12.13_spmd, body=%wide.region_11.12_spmd.sunk | while | flops 131074 | bytes 2097253 | solution.py:152
  347.4 5.9 collective-permute-done
  353.4 4.4 collective-permute-start
  357.8 6.2 collective-permute-done
  364.1 4.4 collective-permute-start
  368.5 5.4 collective-permute-done
  373.9 4.4 collective-permute-start
  378.3 4.5 collective-permute-done
  382.9 4.4 collective-permute-start
  387.3 3.9 collective-permute-done
  391.2 5.1 collective-permute-start
  396.4 4.8 collective-permute-done
  401.2 5.6 collective-permute-start
  406.9 3.9 collective-permute-done
  410.8 6.5 collective-permute-start
  417.3 3.9 collective-permute-done
  421.2 6.5 collective-permute-start
  427.7 3.9 collective-permute-done
  431.6 6.5 collective-permute-start
  438.1 3.9 collective-permute-done
  442.0 6.5 collective-permute-start
  448.5 4.1 collective-permute-done
  452.7 6.8 collective-permute-start
  459.5 5.2 collective-permute-done
  464.8 7.1 collective-permute-start
  471.9 6.4 collective-permute-done
  478.3 7.4 collective-permute-start
  485.7 3.9 collective-permute-done
  489.6 6.5 collective-permute-start
  496.1 3.9 collective-permute-done
  501.5 35.9 %while.34 = (s32[]{:T(128)}, f32[16,1,8,4096]{3,2,1,0:T(8,128)}, f32[16,1,8,16]{3,2,1,0:T(8,128)S(1)}, f32[16,1,8,4096]{3,2,1,0:T(8,128)}, f32[16,4096]{1,0:T(8,128)S(1)}, /*index=5*/f32[16,4096]{1,0:T(8,128)S(1)}, s32[]{:T(128)}) while((s32[]{:T(128)}, f32[16,1,8,4096]{3,2,1,0:T(8,128)}, f32[16,1,8,16]{3,2,1,0:T(8,128)S(1)}, ...), condition=%wide.region_15.16_spmd, body=%wide.region_13.15_spmd.sunk | while | flops 2064386 | bytes 1312853 | solution.py:65
  542.8 16.9 %all-to-all-start.2 = ((bf16[128,16,256]{2,0,1:T(8,128)(2,1)}), bf16[128,16,256]{2,0,1:T(8,128)(2,1)S(1)}, u32[]{:S(2)}, u32[]{:S(2)}) async-start(bf16[128,16,256]{2,0,1:T(8,128)(2,1)} %fusion.30), calls=%async_computation.2 | async-start | bytes 2097152 | tf_op jit(solution)/shard_map/all_to_all | solution.py:159
  560.9 12.2 %all-to-all-done.2 = bf16[128,16,256]{2,0,1:T(8,128)(2,1)S(1)} async-done(((bf16[128,16,256]{2,0,1:T(8,128)(2,1)}), bf16[128,16,256]{2,0,1:T(8,128)(2,1)S(1)}, u32[]{:S(2)}, u32[]{:S(2)}) %all-to-all-start.2) | async-done | bytes 1048608 | tf_op jit(solution)/shard_map/all_to_all | solution.py:159
  575.5 6.8 convolution_convert_fusion
  582.9 65.8 %all-reduce.3.cloned.1.call-done = bf16[16,4096]{1,0:T(8,128)(2,1)} async-done(((bf16[16,4096]{1,0:T(8,128)(2,1)}), bf16[16,4096]{1,0:T(8,128)(2,1)}) %all-reduce.3.cloned.1.call-update) | async-done | bytes 131088 | tf_op jit(solution)/shard_map/psum | solution.py:18
  649.5 13.0 %all-gather = f32[128,256]{1,0:T(8,128)S(1)} all-gather(f32[16,256]{1,0:T(8,128)S(1)} %dynamic-slice_convert_fusion), channel_id=2, replica_groups=mesh['req'=8,'seq'=16] {'req'}, dimensions={0}, use_global_device_ids=true | all-gather | bytes 147456 | tf_op jit(solution)/shard_map/all_gather | solution.py:169
  663.2 74.4 %reduce-scatter.2.cloned.1.call-done = bf16[128,2048]{1,0:T(8,128)(2,1)} async-done(((bf16[2048,2048]{1,0:T(8,128)(2,1)}), bf16[128,2048]{1,0:T(8,128)(2,1)}) %reduce-scatter.2.cloned.1.call-update) | async-done | bytes 524304 | tf_op jit(solution)/shard_map/reduce_scatter | solution.py:163
  (345 shorter events, 152.7 us)
Async XLA Ops:
  7.2 115.5 %copy-start = (bf16[256,160]{0,1:T(8,128)(2,1)S(1)}, bf16[256,160]{0,1:T(8,128)(2,1)}, u32[]{:S(2)}) copy-start(bf16[256,160]{0,1:T(8,128)(2,1)} %param.26) | copy-start | bytes 245764
  7.2 4.8 copy-start.10
  7.2 4.8 copy-start.8
  7.2 30.3 %all-gather.7.cloned.1.call-start = ((), (), s32[]{:S(2)}) async-start(), calls=%async_computation.5 | async-start | bytes 2359296 | tf_op jit(solution)/shard_map/all_gather | solution.py:95
  7.9 103.6 %all-gather.5.cloned.1.call-start = ((), (), s32[]{:S(2)}) async-start(), calls=%async_computation.4 | async-start | bytes 8912896 | tf_op jit(solution)/shard_map/all_gather | solution.py:98
  118.4 2.0 copy-start.4
  124.4 30.4 %collective-permute-start.1 = (f32[2048,160]{0,1:T(8,128)S(1)}, f32[2048,160]{0,1:T(8,128)S(1)}, u32[]{:S(2)}, u32[]{:S(2)}) collective-permute-start(f32[2048,160]{0,1:T(8,128)S(1)} %fusion.56), channel_id=1, source_target_pairs={{0,1},{1,0},{2,3},{3,2},{4,5},{5,4},{6,7},{7,6},{8,9},{9,8},{10,11... | collective-permute-start | bytes 3932168 | tf_op jit(solution)/shard_map/ppermute | solution.py:120
  155.0 31.1 %collective-permute-start.2 = (f32[2048,160]{0,1:T(8,128)S(1)}, f32[2048,160]{0,1:T(8,128)S(1)}, u32[]{:S(2)}, u32[]{:S(2)}) collective-permute-start(f32[2048,160]{0,1:T(8,128)S(1)} %add.139), channel_id=1, source_target_pairs={{0,2},{1,3},{2,0},{3,1},{4,6},{5,7},{6,4},{7,5},{8,10},{9,11},{10,... | collective-permute-start | bytes 3932168 | tf_op jit(solution)/shard_map/ppermute | solution.py:120
  186.3 36.5 %copy-start.11 = (bf16[256]{0:T(256)(128)(2,1)S(1)}, bf16[256]{0:T(256)(128)(2,1)}, u32[]{:S(2)}) copy-start(bf16[256]{0:T(256)(128)(2,1)} %param.28) | copy-start | bytes 1540
  186.3 36.5 %copy-start.12 = (s32[8]{0:T(128)S(1)}, s32[8]{0:T(128)}, u32[]{:S(2)}) copy-start(s32[8]{0:T(128)} %param.20) | copy-start | bytes 100
  186.3 28.7 %collective-permute-start.3 = (f32[2048,160]{0,1:T(8,128)S(1)}, f32[2048,160]{0,1:T(8,128)S(1)}, u32[]{:S(2)}, u32[]{:S(2)}) collective-permute-start(f32[2048,160]{0,1:T(8,128)S(1)} %add.140), channel_id=1, source_target_pairs={{0,4},{1,5},{2,6},{3,7},{4,0},{5,1},{6,2},{7,3},{8,12},{9,13},{10,... | collective-permute-start | bytes 3932168 | tf_op jit(solution)/shard_map/ppermute | solution.py:120
  215.2 40.1 %collective-permute-start.4 = (f32[2048,160]{0,1:T(8,128)S(1)}, f32[2048,160]{0,1:T(8,128)}, u32[]{:S(2)}, u32[]{:S(2)}) collective-permute-start(f32[2048,160]{0,1:T(8,128)S(1)} %add.141), channel_id=1, source_target_pairs={{0,8},{1,9},{2,10},{3,11},{4,12},{5,13},{6,14},{7,15},{8,0},{9,1},... | collective-permute-start | bytes 3932168 | tf_op jit(solution)/shard_map/ppermute | solution.py:120
  218.2 41.4 %all-to-all-start.1 = ((bf16[16,128,256]{2,1,0:T(8,128)(2,1)}), bf16[16,128,256]{2,1,0:T(8,128)(2,1)S(1)}, u32[]{:S(2)}, u32[]{:S(2)}) async-start(bf16[16,128,256]{2,1,0:T(8,128)(2,1)} %bitcast.17), calls=%async_computation.1 | async-start | bytes 2097152 | tf_op jit(solution)/shard_map/all_to_all | solution.py:135
  222.8 33.9 %copy-start.9 = (bf16[128,256]{1,0:T(8,128)(2,1)S(1)}, bf16[128,256]{1,0:T(8,128)(2,1)}, u32[]{:S(2)}) copy-start(bf16[128,256]{1,0:T(8,128)(2,1)} %param.27) | copy-start | bytes 196612
  256.7 1.5 copy-start.5
  258.2 7.5 %copy-start.7 = (f32[4096]{0:T(1024)S(1)}, f32[4096]{0:T(1024)}, u32[]{:S(2)}) copy-start(f32[4096]{0:T(1024)} %param.30) | copy-start | bytes 49156
  259.6 19.2 %all-to-all-start = ((bf16[16,128,256]{1,2,0:T(8,128)(2,1)}), bf16[16,128,256]{1,2,0:T(8,128)(2,1)S(1)}, u32[]{:S(2)}, u32[]{:S(2)}) async-start(bf16[16,128,256]{1,2,0:T(8,128)(2,1)} %copy.43), calls=%async_computation | async-start | bytes 2097152 | tf_op jit(solution)/shard_map/all_to_all | solution.py:136
  264.9 310.5 %all-gather.9.cloned.1.call-start = ((), (), s32[]{:S(2)}) async-start(), calls=%async_computation.6 | async-start | bytes 1179648 | tf_op jit(solution)/shard_map/all_gather | solution.py:134
  286.3 1.8 copy-start.6
  286.7 1.4 copy-start.3
  345.0 8.4 %collective-permute-start = (f32[16,4096]{1,0:T(8,128)S(1)}, f32[16,4096]{1,0:T(8,128)S(1)}, u32[]{:S(2)}, u32[]{:S(2)}) collective-permute-start(f32[16,4096]{1,0:T(8,128)S(1)} %bitcast_add_fusion.3), channel_id=1, source_target_pairs={{0,1},{1,2},{2,3},{3,4},{4,5},{5,6},{6,7},{7,8},{8,9},{9,10},{10,1... | collective-permute-start | bytes 786440 | tf_op jit(solution)/shard_map/while/body/eval_jaxpr/ppermute | solution.py:13
  353.4 10.7 %collective-permute-start = (f32[16,4096]{1,0:T(8,128)S(1)}, f32[16,4096]{1,0:T(8,128)S(1)}, u32[]{:S(2)}, u32[]{:S(2)}) collective-permute-start(f32[16,4096]{1,0:T(8,128)S(1)} %bitcast_add_fusion.3), channel_id=1, source_target_pairs={{0,1},{1,2},{2,3},{3,4},{4,5},{5,6},{6,7},{7,8},{8,9},{9,10},{10,1... | collective-permute-start | bytes 786440 | tf_op jit(solution)/shard_map/while/body/eval_jaxpr/ppermute | solution.py:13
  364.1 9.8 %collective-permute-start = (f32[16,4096]{1,0:T(8,128)S(1)}, f32[16,4096]{1,0:T(8,128)S(1)}, u32[]{:S(2)}, u32[]{:S(2)}) collective-permute-start(f32[16,4096]{1,0:T(8,128)S(1)} %bitcast_add_fusion.3), channel_id=1, source_target_pairs={{0,1},{1,2},{2,3},{3,4},{4,5},{5,6},{6,7},{7,8},{8,9},{9,10},{10,1... | collective-permute-start | bytes 786440 | tf_op jit(solution)/shard_map/while/body/eval_jaxpr/ppermute | solution.py:13
  373.9 8.9 %collective-permute-start = (f32[16,4096]{1,0:T(8,128)S(1)}, f32[16,4096]{1,0:T(8,128)S(1)}, u32[]{:S(2)}, u32[]{:S(2)}) collective-permute-start(f32[16,4096]{1,0:T(8,128)S(1)} %bitcast_add_fusion.3), channel_id=1, source_target_pairs={{0,1},{1,2},{2,3},{3,4},{4,5},{5,6},{6,7},{7,8},{8,9},{9,10},{10,1... | collective-permute-start | bytes 786440 | tf_op jit(solution)/shard_map/while/body/eval_jaxpr/ppermute | solution.py:13
  382.9 8.3 %collective-permute-start = (f32[16,4096]{1,0:T(8,128)S(1)}, f32[16,4096]{1,0:T(8,128)S(1)}, u32[]{:S(2)}, u32[]{:S(2)}) collective-permute-start(f32[16,4096]{1,0:T(8,128)S(1)} %bitcast_add_fusion.3), channel_id=1, source_target_pairs={{0,1},{1,2},{2,3},{3,4},{4,5},{5,6},{6,7},{7,8},{8,9},{9,10},{10,1... | collective-permute-start | bytes 786440 | tf_op jit(solution)/shard_map/while/body/eval_jaxpr/ppermute | solution.py:13
  391.2 10.0 %collective-permute-start = (f32[16,4096]{1,0:T(8,128)S(1)}, f32[16,4096]{1,0:T(8,128)S(1)}, u32[]{:S(2)}, u32[]{:S(2)}) collective-permute-start(f32[16,4096]{1,0:T(8,128)S(1)} %bitcast_add_fusion.3), channel_id=1, source_target_pairs={{0,1},{1,2},{2,3},{3,4},{4,5},{5,6},{6,7},{7,8},{8,9},{9,10},{10,1... | collective-permute-start | bytes 786440 | tf_op jit(solution)/shard_map/while/body/eval_jaxpr/ppermute | solution.py:13
  401.2 9.5 %collective-permute-start = (f32[16,4096]{1,0:T(8,128)S(1)}, f32[16,4096]{1,0:T(8,128)S(1)}, u32[]{:S(2)}, u32[]{:S(2)}) collective-permute-start(f32[16,4096]{1,0:T(8,128)S(1)} %bitcast_add_fusion.3), channel_id=1, source_target_pairs={{0,1},{1,2},{2,3},{3,4},{4,5},{5,6},{6,7},{7,8},{8,9},{9,10},{10,1... | collective-permute-start | bytes 786440 | tf_op jit(solution)/shard_map/while/body/eval_jaxpr/ppermute | solution.py:13
  410.8 10.4 %collective-permute-start = (f32[16,4096]{1,0:T(8,128)S(1)}, f32[16,4096]{1,0:T(8,128)S(1)}, u32[]{:S(2)}, u32[]{:S(2)}) collective-permute-start(f32[16,4096]{1,0:T(8,128)S(1)} %bitcast_add_fusion.3), channel_id=1, source_target_pairs={{0,1},{1,2},{2,3},{3,4},{4,5},{5,6},{6,7},{7,8},{8,9},{9,10},{10,1... | collective-permute-start | bytes 786440 | tf_op jit(solution)/shard_map/while/body/eval_jaxpr/ppermute | solution.py:13
  421.2 10.4 %collective-permute-start = (f32[16,4096]{1,0:T(8,128)S(1)}, f32[16,4096]{1,0:T(8,128)S(1)}, u32[]{:S(2)}, u32[]{:S(2)}) collective-permute-start(f32[16,4096]{1,0:T(8,128)S(1)} %bitcast_add_fusion.3), channel_id=1, source_target_pairs={{0,1},{1,2},{2,3},{3,4},{4,5},{5,6},{6,7},{7,8},{8,9},{9,10},{10,1... | collective-permute-start | bytes 786440 | tf_op jit(solution)/shard_map/while/body/eval_jaxpr/ppermute | solution.py:13
  431.6 10.4 %collective-permute-start = (f32[16,4096]{1,0:T(8,128)S(1)}, f32[16,4096]{1,0:T(8,128)S(1)}, u32[]{:S(2)}, u32[]{:S(2)}) collective-permute-start(f32[16,4096]{1,0:T(8,128)S(1)} %bitcast_add_fusion.3), channel_id=1, source_target_pairs={{0,1},{1,2},{2,3},{3,4},{4,5},{5,6},{6,7},{7,8},{8,9},{9,10},{10,1... | collective-permute-start | bytes 786440 | tf_op jit(solution)/shard_map/while/body/eval_jaxpr/ppermute | solution.py:13
  442.0 10.6 %collective-permute-start = (f32[16,4096]{1,0:T(8,128)S(1)}, f32[16,4096]{1,0:T(8,128)S(1)}, u32[]{:S(2)}, u32[]{:S(2)}) collective-permute-start(f32[16,4096]{1,0:T(8,128)S(1)} %bitcast_add_fusion.3), channel_id=1, source_target_pairs={{0,1},{1,2},{2,3},{3,4},{4,5},{5,6},{6,7},{7,8},{8,9},{9,10},{10,1... | collective-permute-start | bytes 786440 | tf_op jit(solution)/shard_map/while/body/eval_jaxpr/ppermute | solution.py:13
  452.7 12.0 %collective-permute-start = (f32[16,4096]{1,0:T(8,128)S(1)}, f32[16,4096]{1,0:T(8,128)S(1)}, u32[]{:S(2)}, u32[]{:S(2)}) collective-permute-start(f32[16,4096]{1,0:T(8,128)S(1)} %bitcast_add_fusion.3), channel_id=1, source_target_pairs={{0,1},{1,2},{2,3},{3,4},{4,5},{5,6},{6,7},{7,8},{8,9},{9,10},{10,1... | collective-permute-start | bytes 786440 | tf_op jit(solution)/shard_map/while/body/eval_jaxpr/ppermute | solution.py:13
  464.8 13.5 %collective-permute-start = (f32[16,4096]{1,0:T(8,128)S(1)}, f32[16,4096]{1,0:T(8,128)S(1)}, u32[]{:S(2)}, u32[]{:S(2)}) collective-permute-start(f32[16,4096]{1,0:T(8,128)S(1)} %bitcast_add_fusion.3), channel_id=1, source_target_pairs={{0,1},{1,2},{2,3},{3,4},{4,5},{5,6},{6,7},{7,8},{8,9},{9,10},{10,1... | collective-permute-start | bytes 786440 | tf_op jit(solution)/shard_map/while/body/eval_jaxpr/ppermute | solution.py:13
  478.3 11.3 %collective-permute-start = (f32[16,4096]{1,0:T(8,128)S(1)}, f32[16,4096]{1,0:T(8,128)S(1)}, u32[]{:S(2)}, u32[]{:S(2)}) collective-permute-start(f32[16,4096]{1,0:T(8,128)S(1)} %bitcast_add_fusion.3), channel_id=1, source_target_pairs={{0,1},{1,2},{2,3},{3,4},{4,5},{5,6},{6,7},{7,8},{8,9},{9,10},{10,1... | collective-permute-start | bytes 786440 | tf_op jit(solution)/shard_map/while/body/eval_jaxpr/ppermute | solution.py:13
  489.6 10.4 %collective-permute-start = (f32[16,4096]{1,0:T(8,128)S(1)}, f32[16,4096]{1,0:T(8,128)S(1)}, u32[]{:S(2)}, u32[]{:S(2)}) collective-permute-start(f32[16,4096]{1,0:T(8,128)S(1)} %bitcast_add_fusion.3), channel_id=1, source_target_pairs={{0,1},{1,2},{2,3},{3,4},{4,5},{5,6},{6,7},{7,8},{8,9},{9,10},{10,1... | collective-permute-start | bytes 786440 | tf_op jit(solution)/shard_map/while/body/eval_jaxpr/ppermute | solution.py:13
  542.8 30.3 %all-to-all-start.2 = ((bf16[128,16,256]{2,0,1:T(8,128)(2,1)}), bf16[128,16,256]{2,0,1:T(8,128)(2,1)S(1)}, u32[]{:S(2)}, u32[]{:S(2)}) async-start(bf16[128,16,256]{2,0,1:T(8,128)(2,1)} %fusion.30), calls=%async_computation.2 | async-start | bytes 2097152 | tf_op jit(solution)/shard_map/all_to_all | solution.py:159
  559.8 89.0 %all-reduce.3.cloned.1.call-start = ((), (), s32[]{:S(2)}) async-start(), calls=%async_computation.8 | async-start | bytes 262144 | tf_op jit(solution)/shard_map/psum | solution.py:18
  560.6 176.9 %reduce-scatter.2.cloned.1.call-start = ((), (), s32[]{:S(2)}) async-start(), calls=%async_computation.7 | async-start | bytes 8912896 | tf_op jit(solution)/shard_map/reduce_scatter | solution.py:163
  582.3 0.7 copy-start.13
  582.3 155.3 %copy-start.2 = (bf16[1,128,2048]{2,1,0:T(8,128)(2,1)S(1)}, bf16[1,128,2048]{2,1,0:T(8,128)(2,1)}, u32[]{:S(2)}) copy-start(bf16[1,128,2048]{2,1,0:T(8,128)(2,1)} %param.19) | copy-start | bytes 1572868
  582.3 157.2 %copy-start.1 = (bf16[256,160]{0,1:T(8,128)(2,1)S(1)}, bf16[256,160]{0,1:T(8,128)(2,1)}, u32[]{:S(2)}) copy-start(bf16[256,160]{0,1:T(8,128)(2,1)} %param.26) | copy-start | bytes 245764
Sparse Core Ops, SparseCore 0:
  9.7 27.7 all-gather.6
  40.2 71.2 all-gather.4
  267.4 24.7 all-gather.8
  564.0 84.6 all-reduce.2
  652.0 85.4 reduce-scatter.1
